TPU v7x, 128 devices: a whole 4x4x4 slice. The times are simulated.
128 devices in a mesh: child: 2 (over z_hi), row: 8 (over y, core), col: 8 (over x, z_lo).
Axes of the slice: x: 4, y: 4, z: 4 (z_hi: 2, z_lo: 2; z = z_hi * 2 + z_lo), core: 2. Of those that a mesh axis runs over, the one named last changes fastest.
Arguments:
- child_fronts: float32 [2, 8192, 8192], P('child', 'row', 'col')
- parent_front: float32 [12288, 12288], P('row', ('child', 'col')), may hold values from -6 to 6
- index_maps: int32 [2, 8192], replicated, may hold values from 0 to 12287, as said below
- orders: int32 [2], replicated, may hold values from 4096 to 8192, as said below
Outputs:
- assembled: float32 [12288, 12288], P('row', ('child', 'col'))
- panel_factor: float32 [2, 8192, 512], P('child', 'row')
Inputs may be any that keep to these rules, and one draw needn't show every extreme that they name: For each child, index_maps is one to one. Cut the child indices into aligned blocks of 8192 / 8 and the parent indices into 2 * 8 aligned slices of 12288 / (2 * 8): each block sends exactly 8192 / (2 * 8 * 8) of its indices into each slice. `orders`: one child's order is 8192.
All inputs are finite; a program needn't handle non-finite values.
Results may differ from a plain program's by a relative error of at most 0.0001.
Values sent between devices are 32-bit elements; how exact they have to be, the bound alone decides.
No kernel may reach another device: no remote copies, remote signals or barrier semaphores. Data moves between devices by JAX's collectives and lax.ppermute only.
A program may use at most 128 MiB of HBM per device.

v0:
```python
import jax
import jax.numpy as jnp
from jax import lax
from jax.sharding import PartitionSpec as P

PANEL = 512
FRONT = 8192


def from_root(value, axis, source):
    kept = jnp.where(lax.axis_index(axis) == source, value, 0).astype(value.dtype)
    return lax.psum(kept, axis)


def select_rows(parent_map, owner, width, count):
    everywhere = jnp.arange(FRONT, dtype=jnp.int32)
    keyed = jnp.where(parent_map // width == owner, everywhere, everywhere + FRONT)
    chosen = jnp.argsort(keyed)[:count]
    return parent_map[chosen] - owner * width


def invert_slots(slots, length):
    count = slots.shape[0]
    lookup = jnp.full((length,), count, jnp.int32)
    return lookup.at[slots].set(jnp.arange(count, dtype=jnp.int32))


def factor_panel(corner, columns, global_rows, own_order):
    diag_factor = jnp.linalg.cholesky(corner)
    solved = lax.linalg.triangular_solve(
        diag_factor, columns, left_side=False, lower=True, transpose_a=True
    )
    top_rows = jnp.pad(diag_factor, ((0, columns.shape[0] - PANEL), (0, 0)))
    result = jnp.where(global_rows[:, None] < PANEL, top_rows, solved)
    return jnp.where(global_rows[:, None] < own_order, result, jnp.float32(0.0))


def on_device(child_fronts, parent_front, index_maps, orders):
    block_here = child_fronts[0]
    rows_here, cols_here = block_here.shape
    child_index = lax.axis_index("child")
    row_index = lax.axis_index("row")
    col_index = lax.axis_index("col")
    n_row = lax.axis_size("row")
    n_col = lax.axis_size("col")
    own_map = lax.dynamic_index_in_dim(index_maps, child_index, 0, keepdims=False)
    own_order = lax.dynamic_index_in_dim(orders, child_index, 0, keepdims=False)
    global_rows = row_index * rows_here + jnp.arange(rows_here, dtype=jnp.int32)
    global_cols = col_index * cols_here + jnp.arange(cols_here, dtype=jnp.int32)
    corner = from_root(block_here[:PANEL, :PANEL], ("row", "col"), 0)
    columns = from_root(block_here[:, :PANEL], "col", 0)
    own_panel = factor_panel(corner, columns, global_rows, own_order)
    other_panel = from_root(own_panel, "row", col_index)
    update = block_here - jnp.dot(own_panel, other_panel.T, precision=lax.Precision.HIGHEST)
    live_rows = (global_rows >= PANEL) & (global_rows < own_order)
    live_cols = (global_cols >= PANEL) & (global_cols < own_order)
    update = jnp.where(live_rows[:, None] & live_cols[None, :], update, jnp.float32(0.0))
    parent_rows, parent_cols = parent_front.shape
    row_map = lax.dynamic_slice_in_dim(own_map, row_index * rows_here, rows_here)
    col_map = lax.dynamic_slice_in_dim(own_map, col_index * cols_here, cols_here)
    row_keys = row_map // parent_rows * rows_here + jnp.arange(rows_here, dtype=jnp.int32)
    col_keys = col_map // parent_cols * cols_here + jnp.arange(cols_here, dtype=jnp.int32)
    sorted_block = update[jnp.argsort(row_keys)][:, jnp.argsort(col_keys)]
    part_rows = rows_here // n_row
    part_cols = cols_here // (2 * n_col)
    pieces = (
        sorted_block.reshape(n_row, part_rows, 2, n_col, part_cols)
        .transpose(2, 0, 3, 1, 4)
        .reshape(-1, part_cols)
    )
    arrived = lax.all_to_all(
        pieces, ("child", "row", "col"), split_axis=0, concat_axis=0, tiled=True
    )
    arrived = (
        arrived.reshape(2, n_row, n_col, part_rows, part_cols)
        .transpose(0, 1, 3, 2, 4)
        .reshape(2, rows_here, n_col * part_cols)
    )
    col_owner = child_index * n_col + col_index
    assembled = parent_front
    for source in range(2):
        parent_map = index_maps[source]
        row_slots = select_rows(parent_map, row_index, parent_rows, rows_here)
        col_slots = select_rows(parent_map, col_owner, parent_cols, n_col * part_cols)
        row_lookup = invert_slots(row_slots, parent_rows)
        col_lookup = invert_slots(col_slots, parent_cols)
        padded = jnp.pad(arrived[source], ((0, 1), (0, 1)))
        placed = jnp.take(jnp.take(padded, row_lookup, axis=0), col_lookup, axis=1)
        assembled = assembled + placed
    return (assembled, own_panel[None])


def solution(mesh):
    in_specs = (P("child", "row", "col"), P("row", ("child", "col")), P(), P())
    out_specs = (P("row", ("child", "col")), P("child", "row", None))
    return jax.shard_map(
        on_device, mesh=mesh, in_specs=in_specs, out_specs=out_specs, check_vma=False
    )
```

profile of v0, /device:TPU:0, one launch (start us, length us, event | category | flops | bytes accessed | tf_op | source)
XLA Modules:
  0.0 977.2 jit_solution(15241625877835123751)
XLA Ops:
  7.2 5.3 copy.24
  12.6 2.3 slice_select_fusion.1
  14.9 3.2 slice_select_fusion
  20.0 6.8 sort.95
  27.3 6.8 sort.93
  34.7 533.7 %all-reduce.8.cloned.1.call-done = f32[512,512]{0,1:T(8,128)} async-done(((f32[512,512]{0,1:T(8,128)}), f32[512,512]{0,1:T(8,128)}) %all-reduce.8.cloned.1.call-update) | async-done | bytes 1048592 | tf_op jit(solution)/shard_map/psum | solution.py:12
  568.4 1.6 copy.25
  569.9 1.4 fusion.13
  571.4 11.7 %cholesky.103 = f32[128,128]{1,0:T(8,128)S(1)} custom-call(f32[128,128]{1,0:T(8,128)S(1)} %cholesky.263), custom_call_target="Cholesky" | custom-call | tf_op jit(solution)/shard_map/jit(cholesky)/cholesky | solution.py:29
  583.2 10.2 %custom-call.30 = f32[1,128,128]{1,2,0:T(8,128)S(1)} custom-call(f32[1,128,128]{2,1,0:T(8,128)S(1)} %get-tuple-element.63), custom_call_target="InvertDiagBlocksLowerTriangular" | custom-call | tf_op jit(solution)/shard_map/jit(cholesky)/cholesky | solution.py:29
  594.3 11.7 %cholesky.215 = f32[128,128]{1,0:T(8,128)S(1)} custom-call(f32[128,128]{1,0:T(8,128)S(1)} %cholesky.267), custom_call_target="Cholesky" | custom-call | tf_op jit(solution)/shard_map/jit(cholesky)/cholesky | solution.py:29
  606.1 9.8 %custom-call.31 = f32[1,128,128]{1,2,0:T(8,128)S(1)} custom-call(f32[1,128,128]{2,1,0:T(8,128)S(1)} %get-tuple-element.61), custom_call_target="InvertDiagBlocksLowerTriangular" | custom-call | tf_op jit(solution)/shard_map/jit(cholesky)/cholesky | solution.py:29
  617.0 11.9 %cholesky.236 = f32[128,128]{1,0:T(8,128)S(1)} custom-call(f32[128,128]{1,0:T(8,128)S(1)} %cholesky.272), custom_call_target="Cholesky" | custom-call | tf_op jit(solution)/shard_map/jit(cholesky)/cholesky | solution.py:29
  629.0 9.8 %custom-call.32 = f32[1,128,128]{1,2,0:T(8,128)S(1)} custom-call(f32[1,128,128]{2,1,0:T(8,128)S(1)} %get-tuple-element.59), custom_call_target="InvertDiagBlocksLowerTriangular" | custom-call | tf_op jit(solution)/shard_map/jit(cholesky)/cholesky | solution.py:29
  639.6 11.7 %cholesky.253 = f32[128,128]{1,0:T(8,128)S(1)} custom-call(f32[128,128]{1,0:T(8,128)S(1)} %convolution_subtract_fusion.4), custom_call_target="Cholesky" | custom-call | tf_op jit(solution)/shard_map/jit(cholesky)/cholesky | solution.py:29
  656.3 11.0 %while.1 = (s32[]{:T(128)}, f32[512,512]{0,1:T(8,128)S(1)}, s32[4,2]{0,1:T(2,128)S(1)}, f32[4,128,128]{2,1,0:T(8,128)}, s32[]{:T(128)}) while((s32[]{:T(128)}, f32[512,512]{0,1:T(8,128)S(1)}, s32[4,2]{0,1:T(2,128)S(1)}, f32[4,128,128]{2,1,0:T(8,128)}, s32[]{:T(128)}) %tuple.45), condition=%wide.while_cond, body=%wide.while_body.sunk | while | flops 2 | bytes 393329 | solution.py:30
  657.0 1.4 dynamic-slice.9
  659.8 1.4 dynamic-slice.9
  667.3 40.6 %custom-call.33 = f32[4,128,128]{1,2,0:T(8,128)S(1)} custom-call(f32[4,128,128]{2,1,0:T(8,128)} %get-tuple-element.23), custom_call_target="InvertDiagBlocksLowerTriangular" | custom-call | tf_op jit(solution)/shard_map/triangular_solve | solution.py:30
  707.9 1.8 fusion.15
  709.8 1.7 convolution_subtract_fusion.1
  713.4 2.1 fusion.7
  716.2 2.5 fusion.68
  719.4 4.4 sort.90
  723.7 4.4 sort.91
  728.1 6.8 sort.94
  734.9 6.9 sort.92
  742.5 40.9 %all-reduce.12.cloned.1.call-done = f32[1024,512]{0,1:T(8,128)} async-done(((f32[1024,512]{0,1:T(8,128)}), f32[1024,512]{0,1:T(8,128)}) %all-reduce.12.cloned.1.call-update) | async-done | bytes 2097168 | tf_op jit(solution)/shard_map/psum | solution.py:12
  783.4 10.7 %subtract_select_fusion = f32[1024,1024]{0,1:T(8,128)} fusion(f32[1024,512]{0,1:T(8,128)} %all-reduce.12.cloned.1.call-done, pred[1024]{0:T(1024)(128)(4,1)S(1)} %fusion.60, pred[1024]{0:T(1024)(128)(4,1)S(1)} %fusion.61, f32[1,1024,1024]{1,2,0:T(8,128)} %copy.24, f32[1024,128]{0,1:T(8,128)S(1)} %fusion.25, f32[1024,128]{0,1:T(8,128)S(1)} %fusion.26, ...), kind=kOutput, calls=%fused_computation.18 | convolution fusion | flops 6448218112 | bytes 13635584 | tf_op jit(solution)/shard_map/dot_general | solution.py:54
  794.1 5.3 copy.35
  799.5 8.5 gather_fusion
  808.0 5.3 copy.36
  813.3 8.5 gather_fusion.1
  821.9 3.2 copy.55
  825.1 2.8 copy.37
  827.8 8.7 all-to-all-start
  836.6 3.1 gather_fusion.5
  839.8 6.2 gather_fusion.4
  845.9 6.2 gather_fusion.2
  852.1 3.1 gather_fusion.3
  855.3 6.2 copy.41
  861.5 4.3 scatter_custom_fusion.2
  865.9 4.3 scatter_custom_fusion
  870.2 2.4 scatter_custom_fusion.3
  872.7 2.4 scatter_custom_fusion.1
  875.3 2.0 copy.46
  877.4 11.2 %all-to-all-done = f32[128,128,64]{1,2,0:T(8,128)} async-done(((f32[128,128,64]{1,2,0:T(8,128)}), f32[128,128,64]{1,2,0:T(8,128)}, u32[]{:S(2)}, u32[]{:S(2)}) %all-to-all-start) | async-done | bytes 4194336 | tf_op jit(solution)/shard_map/all_to_all | solution.py:71
  888.5 4.0 fusion.71
  892.6 2.7 copy.50
  895.2 4.8 reshape.331
  900.0 1.8 pad.13
  901.8 5.4 gather_fusion.6
  907.2 4.3 broadcast_select_fusion.1
  911.6 3.4 copy.40
  914.9 3.8 copy.51
  918.7 4.8 reshape.332
  923.5 3.3 pad.14
  926.8 7.9 gather_fusion.8
  934.7 4.3 broadcast_select_fusion
  939.0 5.2 copy.44
  944.2 4.1 gather_fusion.7
  948.3 8.0 gather_fusion.9
  956.3 8.0 bitcast_add_fusion
  964.3 6.0 copy.45
  (120 shorter events, 20.8 us)
Async XLA Ops:
  7.2 561.2 %all-reduce.8.cloned.1.call-start = ((), (), s32[]{:S(2)}) async-start(), calls=%async_computation.1 | async-start | bytes 2097152 | tf_op jit(solution)/shard_map/psum | solution.py:12
  14.9 3.4 copy-start.3
  14.9 3.7 copy-start.6
  14.9 693.0 %all-reduce.10.cloned.1.call-start = ((), (), s32[]{:S(2)}) async-start(), calls=%async_computation.2 | async-start | bytes 4194304 | tf_op jit(solution)/shard_map/psum | solution.py:12
  18.2 765.3 %all-reduce.12.cloned.1.call-start = ((), (), s32[]{:S(2)}) async-start(), calls=%async_computation.3 | async-start | bytes 4194304 | tf_op jit(solution)/shard_map/psum | solution.py:12
  667.3 44.7 %copy-start.1 = (f32[512,512]{0,1:T(8,128)}, f32[512,512]{0,1:T(8,128)S(1)}, u32[]{:S(2)}) copy-start(f32[512,512]{0,1:T(8,128)S(1)} %get-tuple-element.132) | copy-start | bytes 3145732
  707.9 4.1 copy-start.2
  827.8 8.7 copy-start.5
  827.8 60.7 %all-to-all-start = ((f32[128,128,64]{1,2,0:T(8,128)}), f32[128,128,64]{1,2,0:T(8,128)}, u32[]{:S(2)}, u32[]{:S(2)}) async-start(f32[128,128,64]{1,2,0:T(8,128)} %bitcast.99), calls=%async_computation | async-start | bytes 8388608 | tf_op jit(solution)/shard_map/all_to_all | solution.py:71
  839.7 12.3 %copy-start.4 = (s32[512]{0:T(512)S(1)}, s32[512]{0:T(512)}, u32[]{:S(2)}) copy-start(s32[512]{0:T(512)} %compare_select_fusion.13) | copy-start | bytes 6148
  855.3 20.1 %copy-start = (f32[1,1024,512]{1,2,0:T(8,128)S(1)}, f32[1,1024,512]{1,2,0:T(8,128)}, u32[]{:S(2)}) copy-start(f32[1,1024,512]{1,2,0:T(8,128)} %get-tuple-element.52) | copy-start | bytes 6291460
Sparse Core Ops, SparseCore 0:
  15.0 553.3 all-reduce.7
  571.6 104.0 all-reduce.9
  718.8 64.5 all-reduce.11
where the time goes:
time: 988 us; the launch traced here: 977 us
  waiting for transfers between devices  586 us (59%)
  other arithmetic  185 us (19%)
  local copies, waits for them, and re-layouts  158 us (16%)
  matrix products  21.1 us (2%)
  between operations  17.4 us (2%)
    psum x3, waiting for transfers between devices, from_root(): return lax.psum(kept, axis)  575 us
    another operation x14, other arithmetic, factor_panel(): diag_factor = jnp.linalg.cholesky(corner)  79 us
    another operation x3, other arithmetic, factor_panel(): lax.linalg.triangular_solve(diag_factor, columns, left_side=False, lower=...  40.8 us
    sort x4, other arithmetic, select_rows(): chosen = jnp.argsort(keyed)[:count]  27.2 us
    gather x4, local copies, waits for them, and re-layouts, on_device(): placed = jnp.take(jnp.take(padded, row_lookup, axis=0), col_lookup, axis=1)  25.4 us
    unnamed x19, local copies, waits for them, and re-layouts  22.8 us
    gather x3, local copies, waits for them, and re-layouts, on_device(): sorted_block = update[jnp.argsort(row_keys)][:, jnp.argsort(col_keys)]  22.4 us
  transfers between devices with their start and end apart: 4, of which 3 were waited for; matrix products, arithmetic and copies ran while one was open for 23% of the time, Pallas kernels for 0%

commit v1 on v0

--- a/solution.py
+++ b/solution.py
@@ -47,8 +47,8 @@
     own_order = lax.dynamic_index_in_dim(orders, child_index, 0, keepdims=False)
     global_rows = row_index * rows_here + jnp.arange(rows_here, dtype=jnp.int32)
     global_cols = col_index * cols_here + jnp.arange(cols_here, dtype=jnp.int32)
-    corner = from_root(block_here[:PANEL, :PANEL], ("row", "col"), 0)
     columns = from_root(block_here[:, :PANEL], "col", 0)
+    corner = from_root(columns[:PANEL], "row", 0)
     own_panel = factor_panel(corner, columns, global_rows, own_order)
     other_panel = from_root(own_panel, "row", col_index)
     update = block_here - jnp.dot(own_panel, other_panel.T, precision=lax.Precision.HIGHEST)

time: 988 us -> 606 us (0.61)
  waiting for transfers between devices: 586 us -> 206 us
    psum x3, waiting for transfers between devices: 575 us -> 195 us  [from_root(): return lax.psum(kept, axis)]
    unnamed x19 -> x17, local copies, waits for them, and re-layouts: 22.8 us -> 22.8 us
  transfers between devices with their start and end apart: 4 -> 4, of which waited for: 3 -> 4; matrix products, arithmetic and copies ran while one was open for 23% -> 14% of each run, Pallas kernels for 0% -> 0%
where the time goes in v1:
time: 606 us; the launch traced here: 599 us
  waiting for transfers between devices  206 us (34%)
  other arithmetic  186 us (31%)
  local copies, waits for them, and re-layouts  159 us (26%)
  matrix products  22.3 us (4%)
  between operations  17.3 us (3%)
  starting transfers between devices  9.03 us (1%)
    psum x3, waiting for transfers between devices, from_root(): return lax.psum(kept, axis)  195 us
    another operation x14, other arithmetic, factor_panel(): diag_factor = jnp.linalg.cholesky(corner)  79.1 us
    another operation x3, other arithmetic, factor_panel(): lax.linalg.triangular_solve(diag_factor, columns, left_side=False, lower=...  40.4 us
    sort x4, other arithmetic, select_rows(): chosen = jnp.argsort(keyed)[:count]  27.4 us
    gather x4, local copies, waits for them, and re-layouts, on_device(): placed = jnp.take(jnp.take(padded, row_lookup, axis=0), col_lookup, axis=1)  25.4 us
    unnamed x17, local copies, waits for them, and re-layouts  22.8 us
    gather x3, local copies, waits for them, and re-layouts, on_device(): sorted_block = update[jnp.argsort(row_keys)][:, jnp.argsort(col_keys)]  22.4 us
    gather x4, local copies, waits for them, and re-layouts, select_rows(): return parent_map[chosen] - owner * width  18.6 us
  transfers between devices with their start and end apart: 4, of which 4 were waited for; matrix products, arithmetic and copies ran while one was open for 14% of the time, Pallas kernels for 0%

profile of v1, /device:TPU:0, one launch (start us, length us, event | category | flops | bytes accessed | tf_op | source)
XLA Modules:
  0.0 598.8 jit_solution(3926736461916187930)
XLA Ops:
  7.2 5.3 copy.24
  12.6 3.2 slice_select_fusion
  16.8 6.8 %sort.95 = (s32[8192]{0:T(1024)}, s32[8192]{0:T(1024)S(1)}) sort(s32[8192]{0:T(1024)S(1)} %get-tuple-element.66, s32[8192]{0:T(1024)S(1)} %iota.168), dimensions={0}, to_apply=%region_19.22 | sort | flops 106496 | bytes 131072 | tf_op jit(solution)/shard_map/jit(argsort)/sort | solution.py:18
  23.5 6.8 %sort.93 = (s32[8192]{0:T(1024)}, s32[8192]{0:T(1024)S(1)}) sort(s32[8192]{0:T(1024)S(1)} %get-tuple-element.69, s32[8192]{0:T(1024)S(1)} %iota.162), dimensions={0}, to_apply=%region_15.17 | sort | flops 106496 | bytes 131072 | tf_op jit(solution)/shard_map/jit(argsort)/sort | solution.py:18
  31.8 91.4 %all-reduce.8.cloned.1.call-done = f32[1024,512]{0,1:T(8,128)} async-done(((f32[1024,512]{0,1:T(8,128)}), f32[1024,512]{0,1:T(8,128)}) %all-reduce.8.cloned.1.call-update) | async-done | bytes 2097168 | tf_op jit(solution)/shard_map/psum | solution.py:12
  123.2 2.3 slice_select_fusion.1
  126.4 62.0 %all-reduce.10.cloned.1.call-done = f32[512,512]{0,1:T(8,128)} async-done(((f32[512,512]{0,1:T(8,128)}), f32[512,512]{0,1:T(8,128)}) %all-reduce.10.cloned.1.call-update) | async-done | bytes 1048592 | tf_op jit(solution)/shard_map/psum | solution.py:12
  188.3 1.6 copy.25
  189.9 1.4 fusion.13
  191.4 11.7 %cholesky.103 = f32[128,128]{1,0:T(8,128)S(1)} custom-call(f32[128,128]{1,0:T(8,128)S(1)} %cholesky.263), custom_call_target="Cholesky" | custom-call | tf_op jit(solution)/shard_map/jit(cholesky)/cholesky | solution.py:29
  203.2 9.8 %custom-call.30 = f32[1,128,128]{1,2,0:T(8,128)S(1)} custom-call(f32[1,128,128]{2,1,0:T(8,128)S(1)} %get-tuple-element.63), custom_call_target="InvertDiagBlocksLowerTriangular" | custom-call | tf_op jit(solution)/shard_map/jit(cholesky)/cholesky | solution.py:29
  213.8 11.7 %cholesky.215 = f32[128,128]{1,0:T(8,128)S(1)} custom-call(f32[128,128]{1,0:T(8,128)S(1)} %cholesky.267), custom_call_target="Cholesky" | custom-call | tf_op jit(solution)/shard_map/jit(cholesky)/cholesky | solution.py:29
  225.7 10.2 %custom-call.31 = f32[1,128,128]{1,2,0:T(8,128)S(1)} custom-call(f32[1,128,128]{2,1,0:T(8,128)S(1)} %get-tuple-element.61), custom_call_target="InvertDiagBlocksLowerTriangular" | custom-call | tf_op jit(solution)/shard_map/jit(cholesky)/cholesky | solution.py:29
  237.0 11.7 %cholesky.236 = f32[128,128]{1,0:T(8,128)S(1)} custom-call(f32[128,128]{1,0:T(8,128)S(1)} %cholesky.272), custom_call_target="Cholesky" | custom-call | tf_op jit(solution)/shard_map/jit(cholesky)/cholesky | solution.py:29
  248.8 9.8 %custom-call.32 = f32[1,128,128]{1,2,0:T(8,128)S(1)} custom-call(f32[1,128,128]{2,1,0:T(8,128)S(1)} %get-tuple-element.59), custom_call_target="InvertDiagBlocksLowerTriangular" | custom-call | tf_op jit(solution)/shard_map/jit(cholesky)/cholesky | solution.py:29
  259.4 11.9 %cholesky.253 = f32[128,128]{1,0:T(8,128)S(1)} custom-call(f32[128,128]{1,0:T(8,128)S(1)} %convolution_subtract_fusion.4), custom_call_target="Cholesky" | custom-call | tf_op jit(solution)/shard_map/jit(cholesky)/cholesky | solution.py:29
  276.5 11.3 %while.1 = (s32[]{:T(128)}, f32[512,512]{0,1:T(8,128)S(1)}, s32[4,2]{0,1:T(2,128)S(1)}, f32[4,128,128]{2,1,0:T(8,128)}, s32[]{:T(128)}) while((s32[]{:T(128)}, f32[512,512]{0,1:T(8,128)S(1)}, s32[4,2]{0,1:T(2,128)S(1)}, f32[4,128,128]{2,1,0:T(8,128)}, s32[]{:T(128)}) %tuple.45), condition=%wide.while_cond, body=%wide.while_body.sunk | while | flops 2 | bytes 393329 | solution.py:30
  287.8 40.2 %custom-call.33 = f32[4,128,128]{1,2,0:T(8,128)S(1)} custom-call(f32[4,128,128]{2,1,0:T(8,128)} %get-tuple-element.23), custom_call_target="InvertDiagBlocksLowerTriangular" | custom-call | tf_op jit(solution)/shard_map/triangular_solve | solution.py:30
  328.0 1.7 fusion.15
  329.7 1.7 convolution_subtract_fusion.1
  332.0 1.8 convolution_subtract_fusion
  334.4 2.3 fusion.7
  337.3 2.5 fusion.68
  340.6 4.4 sort.90
  345.0 4.4 sort.91
  349.4 6.8 %sort.94 = (s32[8192]{0:T(1024)}, s32[8192]{0:T(1024)S(1)}) sort(s32[8192]{0:T(1024)S(1)} %get-tuple-element.67, s32[8192]{0:T(1024)S(1)} %iota.165), dimensions={0}, to_apply=%region_17.20 | sort | flops 106496 | bytes 131072 | tf_op jit(solution)/shard_map/jit(argsort)/sort | solution.py:18
  356.1 7.1 %sort.92 = (s32[8192]{0:T(1024)}, s32[8192]{0:T(1024)S(1)}) sort(s32[8192]{0:T(1024)S(1)} %get-tuple-element.68, s32[8192]{0:T(1024)S(1)} %iota.159), dimensions={0}, to_apply=%region_13.14 | sort | flops 106496 | bytes 131072 | tf_op jit(solution)/shard_map/jit(argsort)/sort | solution.py:18
  364.0 41.3 %all-reduce.12.cloned.1.call-done = f32[1024,512]{0,1:T(8,128)} async-done(((f32[1024,512]{0,1:T(8,128)}), f32[1024,512]{0,1:T(8,128)}) %all-reduce.12.cloned.1.call-update) | async-done | bytes 2097168 | tf_op jit(solution)/shard_map/psum | solution.py:12
  405.3 10.7 %subtract_select_fusion = f32[1024,1024]{0,1:T(8,128)} fusion(f32[1024,512]{0,1:T(8,128)} %all-reduce.12.cloned.1.call-done, pred[1024]{0:T(1024)(128)(4,1)S(1)} %fusion.60, pred[1024]{0:T(1024)(128)(4,1)S(1)} %fusion.61, f32[1,1024,1024]{1,2,0:T(8,128)} %copy.24, f32[1024,128]{0,1:T(8,128)S(1)} %fusion.25, f32[1024,128]{0,1:T(8,128)S(1)} %fusion.26, ...), kind=kOutput, calls=%fused_computation.18 | convolution fusion | flops 6448218112 | bytes 13635584 | tf_op jit(solution)/shard_map/dot_general | solution.py:54
  415.9 5.3 copy.35
  421.3 8.5 %gather_fusion = f32[1024,1024]{1,0:T(8,128)} fusion(f32[1024,1024]{1,0:T(8,128)} %copy.35, s32[1024]{0:T(1024)S(1)} %fusion.47), kind=kCustom, calls=%fused_computation.4 | custom fusion | bytes 8392704 | tf_op jit(solution)/shard_map/gather | solution.py:63
  429.8 5.3 copy.36
  435.2 8.5 %gather_fusion.1 = f32[1024,1024]{1,0:T(8,128)} fusion(f32[1024,1024]{0,1:T(8,128)} %copy.36, s32[1024]{0:T(1024)S(1)} %fusion.48), kind=kCustom, calls=%fused_computation.5 | custom fusion | bytes 8392704 | tf_op jit(solution)/shard_map/gather | solution.py:63
  443.7 3.2 copy.55
  446.9 2.8 copy.37
  449.7 8.7 %all-to-all-start = ((f32[128,128,64]{1,2,0:T(8,128)}), f32[128,128,64]{1,2,0:T(8,128)}, u32[]{:S(2)}, u32[]{:S(2)}) async-start(f32[128,128,64]{1,2,0:T(8,128)} %bitcast.98), calls=%async_computation | async-start | bytes 8388608 | tf_op jit(solution)/shard_map/all_to_all | solution.py:71
  458.4 3.1 gather_fusion.5
  461.6 6.2 %gather_fusion.4 = s32[1024]{0:T(1024)S(1)} fusion(s32[8192]{0:T(1024)S(1)} %bitcast.95, s32[1024]{0:T(1024)S(1)} %fusion.50), kind=kCustom, calls=%fused_computation.8 | custom fusion | bytes 12288 | tf_op jit(solution)/shard_map/gather | solution.py:19
  467.7 6.2 %gather_fusion.2 = s32[1024]{0:T(1024)S(1)} fusion(s32[8192]{0:T(1024)S(1)} %bitcast.91, s32[1024]{0:T(1024)S(1)} %fusion.49), kind=kCustom, calls=%fused_computation.6 | custom fusion | bytes 12288 | tf_op jit(solution)/shard_map/gather | solution.py:19
  473.9 3.1 gather_fusion.3
  477.1 6.2 %copy.41 = f32[1536,768]{0,1:T(8,128)} copy(f32[1536,768]{1,0:T(8,128)} %param.9) | data formatting | bytes 9437184 | tf_op args[1]
  483.3 4.3 scatter_custom_fusion.2
  487.7 4.3 scatter_custom_fusion
  492.0 2.4 scatter_custom_fusion.3
  494.5 2.4 scatter_custom_fusion.1
  497.2 2.0 copy.46
  499.1 11.2 %all-to-all-done = f32[128,128,64]{1,2,0:T(8,128)} async-done(((f32[128,128,64]{1,2,0:T(8,128)}), f32[128,128,64]{1,2,0:T(8,128)}, u32[]{:S(2)}, u32[]{:S(2)}) %all-to-all-start) | async-done | bytes 4194336 | tf_op jit(solution)/shard_map/all_to_all | solution.py:71
  510.4 4.0 fusion.71
  514.4 2.7 copy.50
  517.1 4.8 reshape.331
  521.9 1.8 pad.13
  523.6 5.4 gather_fusion.6
  529.0 4.3 broadcast_select_fusion.1
  533.4 3.4 copy.40
  536.8 3.8 copy.51
  540.5 4.8 reshape.332
  545.4 3.3 pad.14
  548.7 7.9 %gather_fusion.8 = f32[1536,513]{1,0:T(8,128)} fusion(f32[1025,513]{1,0:T(8,128)} %pad.14, s32[2048]{0:T(1024)S(1)} %pad_clamp_fusion), kind=kCustom, calls=%fused_computation.2.clone | custom fusion | bytes 6309888 | tf_op jit(solution)/shard_map/jit(_take)/gather | solution.py:88
  556.5 4.3 broadcast_select_fusion
  560.9 5.2 copy.44
  566.0 4.1 gather_fusion.7
  570.1 8.0 %gather_fusion.9 = f32[768,1536]{1,0:T(8,128)} fusion(f32[1536,513]{0,1:T(8,128)} %copy.44, s32[1024]{0:T(1024)S(1)} %pad_clamp_fusion.2), kind=kCustom, calls=%fused_computation.3.clone | custom fusion | bytes 9440256 | tf_op jit(solution)/shard_map/jit(_take)/gather | solution.py:88
  578.1 8.0 %bitcast_add_fusion = f32[1536,768]{0,1:T(8,128)} fusion(f32[1536,768]{0,1:T(8,128)} %copy.41, f32[768,1536]{1,0:T(8,128)} %gather_fusion.9, f32[768,1536]{1,0:T(8,128)} %gather_fusion.7, pred[768]{0:T(1024)(128)(4,1)S(1)} %compare_and_fusion.2, pred[768]{0:T(1024)(128)(4,1)S(1)} %compare_and_fusion.3), kind=kLoop, calls=%fused_computation.16 | loop fusion | flops 4718592 | bytes 18875904 | tf_op jit(solution)/shard_map/add | solution.py:89
  586.1 6.0 %copy.45 = f32[1536,768]{1,0:T(8,128)} copy(f32[1536,768]{0,1:T(8,128)} %bitcast_add_fusion) | data formatting | bytes 9437184
  (118 shorter events, 23.5 us)
Async XLA Ops:
  7.2 116.1 %all-reduce.8.cloned.1.call-start = ((), (), s32[]{:S(2)}) async-start(), calls=%async_computation.1 | async-start | bytes 4194304 | tf_op jit(solution)/shard_map/psum | solution.py:12
  12.6 3.4 copy-start.5
  12.6 4.0 copy-start.2
  15.8 172.5 %all-reduce.10.cloned.1.call-start = ((), (), s32[]{:S(2)}) async-start(), calls=%async_computation.2 | async-start | bytes 2097152 | tf_op jit(solution)/shard_map/psum | solution.py:12
  125.5 279.7 %all-reduce.12.cloned.1.call-start = ((), (), s32[]{:S(2)}) async-start(), calls=%async_computation.3 | async-start | bytes 4194304 | tf_op jit(solution)/shard_map/psum | solution.py:12
  287.8 44.1 %copy-start.1 = (f32[512,512]{0,1:T(8,128)}, f32[512,512]{0,1:T(8,128)S(1)}, u32[]{:S(2)}) copy-start(f32[512,512]{0,1:T(8,128)S(1)} %get-tuple-element.133) | copy-start | bytes 3145732
  449.7 8.7 %copy-start.3 = (s32[512]{0:T(512)S(1)}, s32[512]{0:T(512)}, u32[]{:S(2)}) copy-start(s32[512]{0:T(512)} %compare_select_fusion.12) | copy-start | bytes 6148
  449.7 60.7 %all-to-all-start = ((f32[128,128,64]{1,2,0:T(8,128)}), f32[128,128,64]{1,2,0:T(8,128)}, u32[]{:S(2)}, u32[]{:S(2)}) async-start(f32[128,128,64]{1,2,0:T(8,128)} %bitcast.98), calls=%async_computation | async-start | bytes 8388608 | tf_op jit(solution)/shard_map/all_to_all | solution.py:71
  461.6 12.3 %copy-start.4 = (s32[512]{0:T(512)S(1)}, s32[512]{0:T(512)}, u32[]{:S(2)}) copy-start(s32[512]{0:T(512)} %compare_select_fusion.13) | copy-start | bytes 6148
  477.1 20.1 %copy-start = (f32[1,1024,512]{1,2,0:T(8,128)S(1)}, f32[1,1024,512]{1,2,0:T(8,128)}, u32[]{:S(2)}) copy-start(f32[1,1024,512]{1,2,0:T(8,128)} %get-tuple-element.52) | copy-start | bytes 6291460
Sparse Core Ops, SparseCore 0:
  15.9 107.2 all-reduce.7
  126.1 62.1 all-reduce.9
  340.0 65.1 all-reduce.11

commit v2 on v1

--- a/solution.py
+++ b/solution.py
@@ -25,11 +25,8 @@
     return lookup.at[slots].set(jnp.arange(count, dtype=jnp.int32))
 
 
-def factor_panel(corner, columns, global_rows, own_order):
-    diag_factor = jnp.linalg.cholesky(corner)
-    solved = lax.linalg.triangular_solve(
-        diag_factor, columns, left_side=False, lower=True, transpose_a=True
-    )
+def factor_panel(diag_factor, inverse, columns, global_rows, own_order):
+    solved = jnp.dot(columns, inverse.T, precision=lax.Precision.HIGHEST)
     top_rows = jnp.pad(diag_factor, ((0, columns.shape[0] - PANEL), (0, 0)))
     result = jnp.where(global_rows[:, None] < PANEL, top_rows, solved)
     return jnp.where(global_rows[:, None] < own_order, result, jnp.float32(0.0))
@@ -48,9 +45,20 @@
     global_rows = row_index * rows_here + jnp.arange(rows_here, dtype=jnp.int32)
     global_cols = col_index * cols_here + jnp.arange(cols_here, dtype=jnp.int32)
     columns = from_root(block_here[:, :PANEL], "col", 0)
-    corner = from_root(columns[:PANEL], "row", 0)
-    own_panel = factor_panel(corner, columns, global_rows, own_order)
-    other_panel = from_root(own_panel, "row", col_index)
+    sent = jnp.concatenate(
+        [
+            jnp.where(row_index == col_index, columns, 0),
+            jnp.where(row_index == 0, columns[:PANEL], 0),
+        ]
+    )
+    received = lax.psum(sent, "row")
+    other_columns, corner = received[:rows_here], received[rows_here:]
+    diag_factor = jnp.linalg.cholesky(corner)
+    inverse = lax.linalg.triangular_solve(
+        diag_factor, jnp.eye(PANEL, dtype=jnp.float32), left_side=True, lower=True
+    )
+    own_panel = factor_panel(diag_factor, inverse, columns, global_rows, own_order)
+    other_panel = factor_panel(diag_factor, inverse, other_columns, global_cols, own_order)
     update = block_here - jnp.dot(own_panel, other_panel.T, precision=lax.Precision.HIGHEST)
     live_rows = (global_rows >= PANEL) & (global_rows < own_order)
     live_cols = (global_cols >= PANEL) & (global_cols < own_order)

time: 606 us -> 561 us (0.926)
  waiting for transfers between devices: 206 us -> 143 us
  other arithmetic: 186 us -> 194 us
    psum x3 -> x1, waiting for transfers between devices: 195 us -> 66.1 us  [from_root(): return lax.psum(kept, axis)]
    psum x0 -> x1, waiting for transfers between devices: none -> 65.4 us  [on_device(): received = lax.psum(sent, 'row')]
    dot_general x0 -> x2, matrix products: none -> 7.15 us  [factor_panel(): solved = jnp.dot(columns, inverse.T, precision=lax.Precision.HIGHEST)]
    unnamed x17 -> x33, local copies, waits for them, and re-layouts: 22.8 us -> 22.5 us
  transfers between devices with their start and end apart: 4 -> 3, of which waited for: 4 -> 3; matrix products, arithmetic and copies ran while one was open for 14% -> 15% of each run, Pallas kernels for 0% -> 0%
where the time goes in v2:
time: 561 us; the launch traced here: 551 us
  other arithmetic  194 us (35%)
  local copies, waits for them, and re-layouts  162 us (29%)
  waiting for transfers between devices  143 us (25%)
  matrix products  25.4 us (5%)
  between operations  17.6 us (3%)
  starting transfers between devices  9.05 us (2%)
    another operation x14, other arithmetic, on_device(): diag_factor = jnp.linalg.cholesky(corner)  81.9 us
    psum x1, waiting for transfers between devices, from_root(): return lax.psum(kept, axis)  66.1 us
    psum x1, waiting for transfers between devices, on_device(): received = lax.psum(sent, 'row')  65.4 us
    another operation x3, other arithmetic, on_device(): lax.linalg.triangular_solve(diag_factor, jnp.eye(PANEL, dtype=jnp.float32...  41.9 us
    sort x4, other arithmetic, select_rows(): chosen = jnp.argsort(keyed)[:count]  27.4 us
    gather x4, local copies, waits for them, and re-layouts, on_device(): placed = jnp.take(jnp.take(padded, row_lookup, axis=0), col_lookup, axis=1)  25.4 us
    unnamed x33, local copies, waits for them, and re-layouts  22.5 us
    gather x3, local copies, waits for them, and re-layouts, on_device(): sorted_block = update[jnp.argsort(row_keys)][:, jnp.argsort(col_keys)]  22.4 us
  transfers between devices with their start and end apart: 3, of which 3 were waited for; matrix products, arithmetic and copies ran while one was open for 15% of the time, Pallas kernels for 0%

profile of v2, /device:TPU:0, one launch (start us, length us, event | category | flops | bytes accessed | tf_op | source)
XLA Modules:
  0.0 550.6 jit_solution(8429926856810007357)
XLA Ops:
  7.2 5.3 copy.25
  12.6 3.2 slice_select_fusion
  16.8 4.4 sort.90
  21.1 4.4 sort.91
  25.7 6.8 %sort.95 = (s32[8192]{0:T(1024)}, s32[8192]{0:T(1024)S(1)}) sort(s32[8192]{0:T(1024)S(1)} %get-tuple-element.64, s32[8192]{0:T(1024)S(1)} %iota.194), dimensions={0}, to_apply=%region_18.21 | sort | flops 106496 | bytes 131072 | tf_op jit(solution)/shard_map/jit(argsort)/sort | solution.py:18
  32.4 6.8 %sort.94 = (s32[8192]{0:T(1024)}, s32[8192]{0:T(1024)S(1)}) sort(s32[8192]{0:T(1024)S(1)} %get-tuple-element.65, s32[8192]{0:T(1024)S(1)} %iota.191), dimensions={0}, to_apply=%region_16.19 | sort | flops 106496 | bytes 131072 | tf_op jit(solution)/shard_map/jit(argsort)/sort | solution.py:18
  39.2 6.8 %sort.92 = (s32[8192]{0:T(1024)}, s32[8192]{0:T(1024)S(1)}) sort(s32[8192]{0:T(1024)S(1)} %get-tuple-element.66, s32[8192]{0:T(1024)S(1)} %iota.185), dimensions={0}, to_apply=%region_12.13 | sort | flops 106496 | bytes 131072 | tf_op jit(solution)/shard_map/jit(argsort)/sort | solution.py:18
  45.9 7.1 %sort.93 = (s32[8192]{0:T(1024)}, s32[8192]{0:T(1024)S(1)}) sort(s32[8192]{0:T(1024)S(1)} %get-tuple-element.67, s32[8192]{0:T(1024)S(1)} %iota.188), dimensions={0}, to_apply=%region_14.16 | sort | flops 106496 | bytes 131072 | tf_op jit(solution)/shard_map/jit(argsort)/sort | solution.py:18
  57.2 66.1 %all-reduce.7.cloned.1.call-done = f32[1024,512]{0,1:T(8,128)} async-done(((f32[1024,512]{0,1:T(8,128)}), f32[1024,512]{0,1:T(8,128)}) %all-reduce.7.cloned.1.call-update) | async-done | bytes 2097168 | tf_op jit(solution)/shard_map/psum | solution.py:12
  124.6 1.8 broadcast_select_fusion.2
  126.4 2.0 pad_maximum_fusion
  131.9 65.4 %all-reduce.9.cloned.1.call-done = f32[1536,512]{0,1:T(8,128)} async-done(((f32[1536,512]{0,1:T(8,128)}), f32[1536,512]{0,1:T(8,128)}) %all-reduce.9.cloned.1.call-update) | async-done | bytes 3145744 | tf_op jit(solution)/shard_map/psum | solution.py:54
  200.4 11.7 %cholesky.103 = f32[128,128]{1,0:T(8,128)S(1)} custom-call(f32[128,128]{1,0:T(8,128)S(1)} %cholesky.263), custom_call_target="Cholesky" | custom-call | tf_op jit(solution)/shard_map/jit(cholesky)/cholesky | solution.py:56
  212.7 9.8 %custom-call.30 = f32[1,128,128]{1,2,0:T(8,128)S(1)} custom-call(f32[1,128,128]{2,1,0:T(8,128)S(1)} %get-tuple-element.61), custom_call_target="InvertDiagBlocksLowerTriangular" | custom-call | tf_op jit(solution)/shard_map/jit(cholesky)/cholesky | solution.py:56
  223.3 11.9 %cholesky.215 = f32[128,128]{1,0:T(8,128)S(1)} custom-call(f32[128,128]{1,0:T(8,128)S(1)} %cholesky.267), custom_call_target="Cholesky" | custom-call | tf_op jit(solution)/shard_map/jit(cholesky)/cholesky | solution.py:56
  235.9 9.8 %custom-call.31 = f32[1,128,128]{1,2,0:T(8,128)S(1)} custom-call(f32[1,128,128]{2,1,0:T(8,128)S(1)} %get-tuple-element.59), custom_call_target="InvertDiagBlocksLowerTriangular" | custom-call | tf_op jit(solution)/shard_map/jit(cholesky)/cholesky | solution.py:56
  246.8 11.7 %cholesky.236 = f32[128,128]{1,0:T(8,128)S(1)} custom-call(f32[128,128]{1,0:T(8,128)S(1)} %cholesky.272), custom_call_target="Cholesky" | custom-call | tf_op jit(solution)/shard_map/jit(cholesky)/cholesky | solution.py:56
  259.2 9.8 %custom-call.32 = f32[1,128,128]{1,2,0:T(8,128)S(1)} custom-call(f32[1,128,128]{2,1,0:T(8,128)S(1)} %get-tuple-element.57), custom_call_target="InvertDiagBlocksLowerTriangular" | custom-call | tf_op jit(solution)/shard_map/jit(cholesky)/cholesky | solution.py:56
  269.9 12.1 %cholesky.253 = f32[128,128]{1,0:T(8,128)S(1)} custom-call(f32[128,128]{1,0:T(8,128)S(1)} %convolution_subtract_fusion.5), custom_call_target="Cholesky" | custom-call | tf_op jit(solution)/shard_map/jit(cholesky)/cholesky | solution.py:56
  289.6 13.9 %while.1 = (s32[]{:T(128)}, f32[512,512]{0,1:T(8,128)}, s32[4,2]{0,1:T(2,128)S(1)}, f32[4,128,128]{2,1,0:T(8,128)}, s32[]{:T(128)}) while((s32[]{:T(128)}, f32[512,512]{0,1:T(8,128)}, s32[4,2]{0,1:T(2,128)S(1)}, f32[4,128,128]{2,1,0:T(8,128)}, s32[]{:T(128)}) %tuple.46), condition=%wide.while_cond, body=%wide.while_body.sunk | while | flops 2 | bytes 393329 | solution.py:57
  290.2 2.2 dynamic-slice.9
  293.7 2.2 dynamic-slice.9
  297.2 2.2 dynamic-slice.9
  300.7 2.1 dynamic-slice.9
  303.5 40.1 %custom-call.33 = f32[4,128,128]{1,2,0:T(8,128)S(1)} custom-call(f32[4,128,128]{2,1,0:T(8,128)} %get-tuple-element.23), custom_call_target="InvertDiagBlocksLowerTriangular" | custom-call | tf_op jit(solution)/shard_map/triangular_solve | solution.py:57
  348.4 1.8 convolution_subtract_fusion.2
  350.6 3.6 fusion.3
  354.3 3.6 fusion
  357.9 9.0 %subtract_select_fusion = f32[1024,1024]{0,1:T(8,128)} fusion(f32[1024,512]{0,1:T(8,128)S(1)} %fusion, f32[1024,512]{0,1:T(8,128)S(1)} %fusion.3, f32[512,512]{0,1:T(8,128)S(1)} %get-tuple-element.47, pred[1024]{0:T(1024)(128)(4,1)S(1)} %get-tuple-element.73, pred[1024]{0:T(1024)(128)(4,1)S(1)} %copy-done.6, pred[1024]{0:T(1024)(128)(4,1)S(1)} %copy-done.9, ...), kind=kOutput, calls=%fused_computation.18 | convolution fusion | flops 6446645248 | bytes 13635584 | tf_op jit(solution)/shard_map/dot_general | solution.py:62
  366.9 5.3 copy.37
  372.3 8.5 %gather_fusion = f32[1024,1024]{1,0:T(8,128)} fusion(f32[1024,1024]{1,0:T(8,128)} %copy.37, s32[1024]{0:T(1024)S(1)} %fusion.51), kind=kCustom, calls=%fused_computation.4 | custom fusion | bytes 8392704 | tf_op jit(solution)/shard_map/gather | solution.py:71
  380.8 5.3 copy.38
  386.2 8.5 %gather_fusion.1 = f32[1024,1024]{1,0:T(8,128)} fusion(f32[1024,1024]{0,1:T(8,128)} %copy.38, s32[1024]{0:T(1024)S(1)} %fusion.52), kind=kCustom, calls=%fused_computation.5 | custom fusion | bytes 8392704 | tf_op jit(solution)/shard_map/gather | solution.py:71
  394.7 3.2 copy.58
  397.9 2.8 copy.39
  400.7 9.0 %all-to-all-start = ((f32[128,128,64]{1,2,0:T(8,128)}), f32[128,128,64]{1,2,0:T(8,128)}, u32[]{:S(2)}, u32[]{:S(2)}) async-start(f32[128,128,64]{1,2,0:T(8,128)} %bitcast.99), calls=%async_computation | async-start | bytes 8388608 | tf_op jit(solution)/shard_map/all_to_all | solution.py:79
  409.7 3.1 gather_fusion.5
  412.8 6.2 %gather_fusion.4 = s32[1024]{0:T(1024)S(1)} fusion(s32[8192]{0:T(1024)S(1)} %bitcast.95, s32[1024]{0:T(1024)S(1)} %fusion.54), kind=kCustom, calls=%fused_computation.8 | custom fusion | bytes 12288 | tf_op jit(solution)/shard_map/gather | solution.py:19
  419.0 6.2 %gather_fusion.2 = s32[1024]{0:T(1024)S(1)} fusion(s32[8192]{0:T(1024)S(1)} %bitcast.91, s32[1024]{0:T(1024)S(1)} %copy-done.5), kind=kCustom, calls=%fused_computation.6 | custom fusion | bytes 12288 | tf_op jit(solution)/shard_map/gather | solution.py:19
  425.2 3.1 gather_fusion.3
  428.3 6.0 %copy.43 = f32[1536,768]{0,1:T(8,128)} copy(f32[1536,768]{1,0:T(8,128)} %param.9) | data formatting | bytes 9437184 | tf_op args[1]
  434.4 4.3 scatter_custom_fusion.2
  438.8 4.5 scatter_custom_fusion
  443.3 2.4 scatter_custom_fusion.3
  445.8 2.4 scatter_custom_fusion.1
  448.5 1.8 copy.48
  450.3 11.3 %all-to-all-done = f32[128,128,64]{1,2,0:T(8,128)} async-done(((f32[128,128,64]{1,2,0:T(8,128)}), f32[128,128,64]{1,2,0:T(8,128)}, u32[]{:S(2)}, u32[]{:S(2)}) %all-to-all-start) | async-done | bytes 4194336 | tf_op jit(solution)/shard_map/all_to_all | solution.py:79
  461.6 4.0 fusion.77
  465.6 2.7 copy.53
  468.3 4.8 reshape.341
  473.1 1.8 pad.14
  474.9 5.4 gather_fusion.6
  480.3 4.3 broadcast_select_fusion.1
  484.6 3.4 copy.42
  488.0 3.8 copy.54
  491.8 4.8 reshape.342
  496.6 3.3 pad.15
  499.9 7.9 %gather_fusion.8 = f32[1536,513]{1,0:T(8,128)} fusion(f32[1025,513]{1,0:T(8,128)} %pad.15, s32[2048]{0:T(1024)S(1)} %pad_clamp_fusion), kind=kCustom, calls=%fused_computation.2.clone | custom fusion | bytes 6309888 | tf_op jit(solution)/shard_map/jit(_take)/gather | solution.py:96
  507.7 4.3 broadcast_select_fusion
  512.1 5.2 copy.46
  517.2 4.1 gather_fusion.7
  521.4 8.0 %gather_fusion.9 = f32[768,1536]{1,0:T(8,128)} fusion(f32[1536,513]{0,1:T(8,128)} %copy.46, s32[1024]{0:T(1024)S(1)} %pad_clamp_fusion.2), kind=kCustom, calls=%fused_computation.3.clone | custom fusion | bytes 9440256 | tf_op jit(solution)/shard_map/jit(_take)/gather | solution.py:96
  529.3 8.0 %bitcast_add_fusion = f32[1536,768]{0,1:T(8,128)} fusion(f32[1536,768]{0,1:T(8,128)} %copy.43, f32[768,1536]{1,0:T(8,128)} %gather_fusion.9, f32[768,1536]{1,0:T(8,128)} %gather_fusion.7, pred[768]{0:T(1024)(128)(4,1)S(1)} %compare_and_fusion.2, pred[768]{0:T(1024)(128)(4,1)S(1)} %compare_and_fusion.3), kind=kLoop, calls=%fused_computation.16 | loop fusion | flops 4718592 | bytes 18875904 | tf_op jit(solution)/shard_map/add | solution.py:97
  537.3 6.0 %copy.47 = f32[1536,768]{1,0:T(8,128)} copy(f32[1536,768]{0,1:T(8,128)} %bitcast_add_fusion) | data formatting | bytes 9437184
  (137 shorter events, 33.7 us)
Async XLA Ops:
  7.2 116.1 %all-reduce.7.cloned.1.call-start = ((), (), s32[]{:S(2)}) async-start(), calls=%async_computation.1 | async-start | bytes 4194304 | tf_op jit(solution)/shard_map/psum | solution.py:12
  12.6 3.3 copy-start.4
  12.6 3.6 copy-start.13
  15.8 181.4 %all-reduce.9.cloned.1.call-start = ((), (), s32[]{:S(2)}) async-start(), calls=%async_computation.2 | async-start | bytes 6291456 | tf_op jit(solution)/shard_map/psum | solution.py:54
  246.2 98.7 %copy-start.3 = (f32[512,512]{1,0:T(8,128)S(1)}, f32[512,512]{1,0:T(8,128)}, u32[]{:S(2)}) copy-start(f32[512,512]{1,0:T(8,128)} %fusion.18) | copy-start | bytes 3145732
  343.6 7.0 %copy-start.2 = (f32[1536,512]{0,1:T(8,128)S(1)}, f32[1536,512]{0,1:T(8,128)}, u32[]{:S(2)}) copy-start(f32[1536,512]{0,1:T(8,128)} %all-reduce.9.cloned.1.call-done) | copy-start | bytes 9437188
  348.0 6.3 %copy-start.1 = (f32[1024,512]{0,1:T(8,128)S(1)}, f32[1024,512]{0,1:T(8,128)}, u32[]{:S(2)}) copy-start(f32[1024,512]{0,1:T(8,128)} %all-reduce.7.cloned.1.call-done) | copy-start | bytes 6291460
  348.0 6.3 %copy-start.11 = (pred[1024]{0:T(1024)(128)(4,1)S(1)}, pred[1024]{0:T(1024)(128)(4,1)}, u32[]{:S(2)}) copy-start(pred[1024]{0:T(1024)(128)(4,1)} %get-tuple-element.70) | copy-start | bytes 3076
  348.0 6.3 %copy-start.12 = (pred[1024]{0:T(1024)(128)(4,1)S(1)}, pred[1024]{0:T(1024)(128)(4,1)}, u32[]{:S(2)}) copy-start(pred[1024]{0:T(1024)(128)(4,1)} %get-tuple-element.71) | copy-start | bytes 3076
  354.2 3.7 copy-start
  354.2 3.7 copy-start.6
  354.2 3.7 copy-start.9
  354.2 3.7 copy-start.10
  400.7 9.0 %copy-start.8 = (s32[512]{0:T(512)S(1)}, s32[512]{0:T(512)}, u32[]{:S(2)}) copy-start(s32[512]{0:T(512)} %compare_select_fusion.12) | copy-start | bytes 6148
  400.7 60.9 %all-to-all-start = ((f32[128,128,64]{1,2,0:T(8,128)}), f32[128,128,64]{1,2,0:T(8,128)}, u32[]{:S(2)}, u32[]{:S(2)}) async-start(f32[128,128,64]{1,2,0:T(8,128)} %bitcast.99), calls=%async_computation | async-start | bytes 8388608 | tf_op jit(solution)/shard_map/all_to_all | solution.py:79
  409.6 9.3 %copy-start.5 = (s32[1024]{0:T(1024)S(1)}, s32[1024]{0:T(1024)}, u32[]{:S(2)}) copy-start(s32[1024]{0:T(1024)} %fusion.53) | copy-start | bytes 12292
  412.8 12.3 %copy-start.7 = (s32[512]{0:T(512)S(1)}, s32[512]{0:T(512)}, u32[]{:S(2)}) copy-start(s32[512]{0:T(512)} %compare_select_fusion.13) | copy-start | bytes 6148
Sparse Core Ops, SparseCore 0:
  15.9 107.2 all-reduce.6
  128.5 68.7 all-reduce.8

commit v3 on v2

--- a/solution.py
+++ b/solution.py
@@ -10,6 +10,20 @@
 def from_root(value, axis, source):
     kept = jnp.where(lax.axis_index(axis) == source, value, 0).astype(value.dtype)
     return lax.psum(kept, axis)
+
+
+def spread_sum(value, axis):
+    count = lax.axis_size(axis)
+    pieces = value.reshape(count, value.shape[0] // count, value.shape[1])
+    arrived = lax.all_to_all(pieces, axis, 0, 0, tiled=True)
+    return lax.all_gather(arrived.sum(0), axis, axis=0, tiled=True)
+
+
+def from_first(value, axis):
+    count = lax.axis_size(axis)
+    pieces = value.reshape(count, value.shape[0] // count, value.shape[1])
+    arrived = lax.all_to_all(pieces, axis, 0, 0, tiled=True)
+    return lax.all_gather(arrived[0], axis, axis=0, tiled=True)
 
 
 def select_rows(parent_map, owner, width, count):
@@ -44,14 +58,14 @@
     own_order = lax.dynamic_index_in_dim(orders, child_index, 0, keepdims=False)
     global_rows = row_index * rows_here + jnp.arange(rows_here, dtype=jnp.int32)
     global_cols = col_index * cols_here + jnp.arange(cols_here, dtype=jnp.int32)
-    columns = from_root(block_here[:, :PANEL], "col", 0)
+    columns = from_first(block_here[:, :PANEL], "col")
     sent = jnp.concatenate(
         [
             jnp.where(row_index == col_index, columns, 0),
             jnp.where(row_index == 0, columns[:PANEL], 0),
         ]
     )
-    received = lax.psum(sent, "row")
+    received = spread_sum(sent, "row")
     other_columns, corner = received[:rows_here], received[rows_here:]
     diag_factor = jnp.linalg.cholesky(corner)
     inverse = lax.linalg.triangular_solve(

time: 561 us -> 536 us (0.955)
  blocking collectives: 0 us -> 74.7 us
  waiting for transfers between devices: 143 us -> 69.3 us
  local copies, waits for them, and re-layouts: 162 us -> 151 us
  other arithmetic: 194 us -> 184 us
    psum x2 -> x0, waiting for transfers between devices: 131 us -> none  [the longest x1 66.1 us: from_root(): return lax.psum(kept, axis)]
    all_to_all x0 -> x2, blocking collectives: none -> 74.7 us  [the longest x1 42.5 us: spread_sum(): arrived = lax.all_to_all(pieces, axis, 0, 0, tiled=True)]
    all_gather x0 -> x2, waiting for transfers between devices: none -> 52 us  [the longest x1 52 us: from_first(): return lax.all_gather(arrived[0], axis, axis=0, tiled=True)]
    unnamed x33 -> x18, local copies, waits for them, and re-layouts: 22.5 us -> 16.1 us
    all_to_all x1, waiting for transfers between devices: 11.3 us -> 17.3 us  [on_device(): lax.all_to_all(pieces, ('child', 'row', 'col'), split_axis=0, concat_axis...]
    another operation x20 -> x12, local copies, waits for them, and re-layouts: 13.8 us -> 13.7 us
  transfers between devices with their start and end apart: 3 -> 3, of which waited for: 3 -> 2; matrix products, arithmetic and copies ran while one was open for 15% -> 15% of each run, Pallas kernels for 0% -> 0%
where the time goes in v3:
time: 536 us; the launch traced here: 530 us
  other arithmetic  184 us (34%)
  local copies, waits for them, and re-layouts  151 us (28%)
  blocking collectives  74.7 us (14%)
  waiting for transfers between devices  69.3 us (13%)
  matrix products  25.2 us (5%)
  between operations  17.4 us (3%)
  starting transfers between devices  8.06 us (2%)
    another operation x14, other arithmetic, on_device(): diag_factor = jnp.linalg.cholesky(corner)  78.9 us
    all_gather x1, waiting for transfers between devices, from_first(): return lax.all_gather(arrived[0], axis, axis=0, tiled=True)  52 us
    all_to_all x1, blocking collectives, spread_sum(): arrived = lax.all_to_all(pieces, axis, 0, 0, tiled=True)  42.5 us
    another operation x3, other arithmetic, on_device(): lax.linalg.triangular_solve(diag_factor, jnp.eye(PANEL, dtype=jnp.float32...  41.8 us
    all_to_all x1, blocking collectives, from_first(): arrived = lax.all_to_all(pieces, axis, 0, 0, tiled=True)  32.2 us
    sort x4, other arithmetic, select_rows(): chosen = jnp.argsort(keyed)[:count]  27.1 us
    gather x4, local copies, waits for them, and re-layouts, on_device(): placed = jnp.take(jnp.take(padded, row_lookup, axis=0), col_lookup, axis=1)  25.4 us
    gather x3, local copies, waits for them, and re-layouts, on_device(): sorted_block = update[jnp.argsort(row_keys)][:, jnp.argsort(col_keys)]  22.5 us
  transfers between devices with their start and end apart: 3, of which 2 were waited for; matrix products, arithmetic and copies ran while one was open for 15% of the time, Pallas kernels for 0%

profile of v3, /device:TPU:0, one launch (start us, length us, event | category | flops | bytes accessed | tf_op | source)
XLA Modules:
  0.0 530.0 jit_solution(5491588675586270342)
XLA Ops:
  7.2 1.8 slice.189
  9.0 32.2 %all_to_all.19 = f32[8,128,512]{2,1,0:T(8,128)S(1)} all-to-all(f32[8,128,512]{2,1,0:T(8,128)S(1)} %bitcast.115), channel_id=1, replica_groups=mesh['child'=2,'row'=8,'col'=8] {'col'}, dimensions={0} | all-to-all | bytes 4194304 | tf_op jit(solution)/shard_map/all_to_all | solution.py:25
  42.0 52.0 %all-gather.6.cloned.1.call-done = f32[1,1024,512]{2,1,0:T(8,128)} async-done(((f32[1,128,512]{2,1,0:T(8,128)}), f32[1,1024,512]{2,1,0:T(8,128)}) %all-gather.6.cloned.1.call-update) | async-done | bytes 2097168 | tf_op jit(solution)/shard_map/all_gather | solution.py:26
  93.9 1.5 fusion.9
  96.4 42.5 %all_to_all.20 = f32[8,192,512]{2,1,0:T(8,128)S(1)} all-to-all(f32[8,192,512]{2,1,0:T(8,128)S(1)} %bitcast.113), channel_id=1, replica_groups=mesh['child'=2,'row'=8,'col'=8] {'row'}, dimensions={0} | all-to-all | bytes 6291456 | tf_op jit(solution)/shard_map/all_to_all | solution.py:18
  140.9 6.8 %sort.94 = (s32[8192]{0:T(1024)}, s32[8192]{0:T(1024)S(1)}) sort(s32[8192]{0:T(1024)S(1)} %get-tuple-element.63, s32[8192]{0:T(1024)S(1)} %iota.191), dimensions={0}, to_apply=%region_15.18 | sort | flops 106496 | bytes 131072 | tf_op jit(solution)/shard_map/jit(argsort)/sort | solution.py:32
  147.6 6.3 %gather_fusion.4 = s32[1024]{0:T(1024)S(1)} fusion(s32[8192]{0:T(1024)S(1)} %bitcast.108, s32[1024]{0:T(1024)S(1)} %fusion.61), kind=kCustom, calls=%fused_computation.8 | custom fusion | bytes 12288 | tf_op jit(solution)/shard_map/gather | solution.py:33
  154.2 4.4 sort.90
  158.6 4.4 sort.91
  163.0 6.8 %sort.95 = (s32[8192]{0:T(1024)}, s32[8192]{0:T(1024)S(1)}) sort(s32[8192]{0:T(1024)S(1)} %get-tuple-element.62, s32[8192]{0:T(1024)S(1)} %iota.194), dimensions={0}, to_apply=%region_17.20 | sort | flops 106496 | bytes 131072 | tf_op jit(solution)/shard_map/jit(argsort)/sort | solution.py:32
  169.8 6.8 %sort.92 = (s32[8192]{0:T(1024)}, s32[8192]{0:T(1024)S(1)}) sort(s32[8192]{0:T(1024)S(1)} %get-tuple-element.66, s32[8192]{0:T(1024)S(1)} %iota.185), dimensions={0}, to_apply=%region_11.12 | sort | flops 106496 | bytes 131072 | tf_op jit(solution)/shard_map/jit(argsort)/sort | solution.py:32
  176.5 6.8 %sort.93 = (s32[8192]{0:T(1024)}, s32[8192]{0:T(1024)S(1)}) sort(s32[8192]{0:T(1024)S(1)} %get-tuple-element.67, s32[8192]{0:T(1024)S(1)} %iota.188), dimensions={0}, to_apply=%region_13.15 | sort | flops 106496 | bytes 131072 | tf_op jit(solution)/shard_map/jit(argsort)/sort | solution.py:32
  188.9 1.4 fusion.10
  190.3 12.1 %cholesky.103 = f32[128,128]{1,0:T(8,128)S(1)} custom-call(f32[128,128]{1,0:T(8,128)S(1)} %cholesky.263), custom_call_target="Cholesky" | custom-call | tf_op jit(solution)/shard_map/jit(cholesky)/cholesky | solution.py:70
  202.6 9.8 %custom-call.30 = f32[1,128,128]{1,2,0:T(8,128)S(1)} custom-call(f32[1,128,128]{2,1,0:T(8,128)S(1)} %get-tuple-element.59), custom_call_target="InvertDiagBlocksLowerTriangular" | custom-call | tf_op jit(solution)/shard_map/jit(cholesky)/cholesky | solution.py:70
  213.1 11.7 %cholesky.215 = f32[128,128]{1,0:T(8,128)S(1)} custom-call(f32[128,128]{1,0:T(8,128)S(1)} %cholesky.267), custom_call_target="Cholesky" | custom-call | tf_op jit(solution)/shard_map/jit(cholesky)/cholesky | solution.py:70
  224.8 10.0 %custom-call.31 = f32[1,128,128]{1,2,0:T(8,128)S(1)} custom-call(f32[1,128,128]{2,1,0:T(8,128)S(1)} %get-tuple-element.56), custom_call_target="InvertDiagBlocksLowerTriangular" | custom-call | tf_op jit(solution)/shard_map/jit(cholesky)/cholesky | solution.py:70
  235.5 11.7 %cholesky.236 = f32[128,128]{1,0:T(8,128)S(1)} custom-call(f32[128,128]{1,0:T(8,128)S(1)} %cholesky.272), custom_call_target="Cholesky" | custom-call | tf_op jit(solution)/shard_map/jit(cholesky)/cholesky | solution.py:70
  247.9 9.8 %custom-call.32 = f32[1,128,128]{1,2,0:T(8,128)S(1)} custom-call(f32[1,128,128]{2,1,0:T(8,128)S(1)} %get-tuple-element.53), custom_call_target="InvertDiagBlocksLowerTriangular" | custom-call | tf_op jit(solution)/shard_map/jit(cholesky)/cholesky | solution.py:70
  258.3 11.7 %cholesky.253 = f32[128,128]{1,0:T(8,128)S(1)} custom-call(f32[128,128]{1,0:T(8,128)S(1)} %convolution_subtract_fusion.5), custom_call_target="Cholesky" | custom-call | tf_op jit(solution)/shard_map/jit(cholesky)/cholesky | solution.py:70
  275.0 13.7 %while.1 = (s32[]{:T(128)}, f32[512,512]{1,0:T(8,128)}, s32[4,2]{0,1:T(2,128)S(1)}, f32[4,128,128]{2,1,0:T(8,128)}, s32[]{:T(128)}) while((s32[]{:T(128)}, f32[512,512]{1,0:T(8,128)}, s32[4,2]{0,1:T(2,128)S(1)}, f32[4,128,128]{2,1,0:T(8,128)}, s32[]{:T(128)}) %tuple.49), condition=%wide.while_cond, body=%wide.while_body.sunk | while | flops 2 | bytes 132205 | solution.py:71
  275.7 2.8 bitcast_dynamic-update-slice_fusion.2
  279.1 2.8 bitcast_dynamic-update-slice_fusion.2
  282.6 2.8 bitcast_dynamic-update-slice_fusion.2
  286.0 2.7 bitcast_dynamic-update-slice_fusion.2
  288.7 40.5 %custom-call.33 = f32[4,128,128]{1,2,0:T(8,128)S(1)} custom-call(f32[4,128,128]{2,1,0:T(8,128)} %get-tuple-element.23), custom_call_target="InvertDiagBlocksLowerTriangular" | custom-call | tf_op jit(solution)/shard_map/triangular_solve | solution.py:71
  332.2 1.3 convolution_subtract_fusion
  333.9 1.6 convolution_subtract_fusion.2
  336.0 3.5 fusion.3
  339.5 3.5 fusion.5
  343.0 9.8 %subtract_select_fusion = f32[1024,1024]{1,0:T(8,128)} fusion(f32[1024,512]{1,0:T(8,128)S(1)} %fusion.3, f32[512,512]{1,0:T(8,128)S(1)} %get-tuple-element.41, pred[1024]{0:T(1024)(128)(4,1)S(1)} %get-tuple-element.75, pred[1024]{0:T(1024)(128)(4,1)S(1)} %get-tuple-element.73, f32[512,1024]{0,1:T(8,128)S(1)} %fusion.5, ...), kind=kOutput, calls=%fused_computation.18 | convolution fusion | flops 6447693824 | bytes 13637632 | tf_op jit(solution)/shard_map/dot_general | solution.py:76
  352.7 8.6 %gather_fusion = f32[1024,1024]{1,0:T(8,128)} fusion(f32[1024,1024]{1,0:T(8,128)} %subtract_select_fusion, s32[1024]{0:T(1024)S(1)} %fusion.58), kind=kCustom, calls=%fused_computation.4 | custom fusion | bytes 8392704 | tf_op jit(solution)/shard_map/gather | solution.py:85
  361.3 5.3 %copy.28 = f32[1024,1024]{0,1:T(8,128)} copy(f32[1024,1024]{1,0:T(8,128)} %gather_fusion) | data formatting | bytes 8388608 | tf_op jit(solution)/shard_map/gather | solution.py:85
  366.7 8.6 %gather_fusion.1 = f32[1024,1024]{1,0:T(8,128)} fusion(f32[1024,1024]{0,1:T(8,128)} %copy.28, s32[1024]{0:T(1024)S(1)} %fusion.59), kind=kCustom, calls=%fused_computation.5 | custom fusion | bytes 8392704 | tf_op jit(solution)/shard_map/gather | solution.py:85
  375.3 3.2 copy.44
  378.5 2.8 copy.29
  381.2 8.0 %all-to-all-start.2 = ((f32[128,128,64]{1,2,0:T(8,128)}), f32[128,128,64]{1,2,0:T(8,128)}, u32[]{:S(2)}, u32[]{:S(2)}) async-start(f32[128,128,64]{1,2,0:T(8,128)} %bitcast.111), calls=%async_computation.2 | async-start | bytes 8388608 | tf_op jit(solution)/shard_map/all_to_all | solution.py:93
  389.2 3.1 gather_fusion.5
  392.4 6.2 %gather_fusion.2 = s32[1024]{0:T(1024)S(1)} fusion(s32[8192]{0:T(1024)S(1)} %bitcast.105, s32[1024]{0:T(1024)S(1)} %fusion.60), kind=kCustom, calls=%fused_computation.6 | custom fusion | bytes 12288 | tf_op jit(solution)/shard_map/gather | solution.py:33
  398.6 3.1 gather_fusion.3
  401.7 6.0 %copy.33 = f32[1536,768]{0,1:T(8,128)} copy(f32[1536,768]{1,0:T(8,128)} %param.9) | data formatting | bytes 9437184 | tf_op args[1]
  407.8 4.3 scatter_custom_fusion.2
  412.1 4.5 scatter_custom_fusion
  416.7 2.4 scatter_custom_fusion.3
  419.2 2.4 scatter_custom_fusion.1
  421.8 2.0 fusion.7
  423.9 17.3 %all-to-all-done.2 = f32[128,128,64]{1,2,0:T(8,128)} async-done(((f32[128,128,64]{1,2,0:T(8,128)}), f32[128,128,64]{1,2,0:T(8,128)}, u32[]{:S(2)}, u32[]{:S(2)}) %all-to-all-start.2) | async-done | bytes 4194336 | tf_op jit(solution)/shard_map/all_to_all | solution.py:93
  441.2 4.0 fusion.84
  445.2 2.7 copy.39
  447.9 4.8 reshape.354
  452.7 1.8 pad.14
  454.5 5.4 %gather_fusion.6 = f32[1536,513]{1,0:T(8,128)} fusion(f32[1025,513]{1,0:T(8,128)S(1)} %pad.14, s32[2048]{0:T(1024)S(1)} %pad_clamp_fusion.1), kind=kCustom, calls=%fused_computation.clone | custom fusion | bytes 6309888 | tf_op jit(solution)/shard_map/jit(_take)/gather | solution.py:110
  459.9 4.3 broadcast_select_fusion.1
  464.2 3.4 copy.32
  467.6 3.8 copy.40
  471.3 4.8 reshape.355
  476.2 3.3 pad.15
  479.5 7.9 %gather_fusion.8 = f32[1536,513]{1,0:T(8,128)} fusion(f32[1025,513]{1,0:T(8,128)} %pad.15, s32[2048]{0:T(1024)S(1)} %pad_clamp_fusion), kind=kCustom, calls=%fused_computation.2.clone | custom fusion | bytes 6309888 | tf_op jit(solution)/shard_map/jit(_take)/gather | solution.py:110
  487.3 4.3 broadcast_select_fusion
  491.7 5.2 copy.36
  496.8 4.1 gather_fusion.7
  500.9 8.0 %gather_fusion.9 = f32[768,1536]{1,0:T(8,128)} fusion(f32[1536,513]{0,1:T(8,128)} %copy.36, s32[1024]{0:T(1024)S(1)} %pad_clamp_fusion.2), kind=kCustom, calls=%fused_computation.3.clone | custom fusion | bytes 9440256 | tf_op jit(solution)/shard_map/jit(_take)/gather | solution.py:110
  508.9 8.0 %bitcast_add_fusion = f32[1536,768]{0,1:T(8,128)} fusion(f32[1536,768]{0,1:T(8,128)} %copy.33, f32[768,1536]{1,0:T(8,128)} %gather_fusion.9, f32[768,1536]{1,0:T(8,128)} %gather_fusion.7, pred[768]{0:T(1024)(128)(4,1)S(1)} %compare_and_fusion.2, pred[768]{0:T(1024)(128)(4,1)S(1)} %compare_and_fusion.3), kind=kLoop, calls=%fused_computation.16 | loop fusion | flops 4718592 | bytes 18875904 | tf_op jit(solution)/shard_map/add | solution.py:111
  516.9 6.0 %copy.37 = f32[1536,768]{1,0:T(8,128)} copy(f32[1536,768]{0,1:T(8,128)} %bitcast_add_fusion) | data formatting | bytes 9437184
  (108 shorter events, 21.2 us)
Async XLA Ops:
  7.2 86.7 %all-gather.6.cloned.1.call-start = ((), (), s32[]{:S(2)}) async-start(), calls=%async_computation.4 | async-start | bytes 2359296 | tf_op jit(solution)/shard_map/all_gather | solution.py:26
  41.9 145.3 %all-gather.4.cloned.1.call-start = ((), (), s32[]{:S(2)}) async-start(), calls=%async_computation.3 | async-start | bytes 3538944 | tf_op jit(solution)/shard_map/all_gather | solution.py:19
  93.9 1.9 copy-start
  138.9 1.2 copy-start.6
  138.9 1.8 copy-start.5
  234.8 95.7 %copy-start.4 = (f32[512,512]{1,0:T(8,128)S(1)}, f32[512,512]{1,0:T(8,128)}, u32[]{:S(2)}) copy-start(f32[512,512]{1,0:T(8,128)} %fusion.25) | copy-start | bytes 3145732
  329.3 6.7 %copy-start.3 = (f32[1536,512]{1,0:T(8,128)S(1)}, f32[1536,512]{1,0:T(8,128)}, u32[]{:S(2)}) copy-start(f32[1536,512]{1,0:T(8,128)} %all-gather.4.cloned.1.call-done) | copy-start | bytes 9437188
  335.5 3.9 copy-start.1
  339.4 3.5 copy-start.2
  381.2 60.0 %all-to-all-start.2 = ((f32[128,128,64]{1,2,0:T(8,128)}), f32[128,128,64]{1,2,0:T(8,128)}, u32[]{:S(2)}, u32[]{:S(2)}) async-start(f32[128,128,64]{1,2,0:T(8,128)} %bitcast.111), calls=%async_computation.2 | async-start | bytes 8388608 | tf_op jit(solution)/shard_map/all_to_all | solution.py:93
Sparse Core Ops, SparseCore 0:
  42.0 51.8 all-gather.5
  140.1 26.6 all-gather.3
